TPU v7x, 128 devices: a whole 4x4x4 slice. The times are simulated.
128 devices in a mesh: tm: 32 (over x, z, core), feat: 4 (over y).
Axes of the slice: x: 4, y: 4, z: 4, core: 2. Of those that a mesh axis runs over, the one named last changes fastest.
Arguments:
- activations: bfloat16 [81920, 2048], P(('tm', 'feat')), may hold values from -19 to 19
- targets: bfloat16 [81920, 128], P(('tm', 'feat')), may hold values from -8 to 8
- span_of: int32 [81920], P(('tm', 'feat')), may hold values from 0 to 31, as said below
Outputs:
- predictions: bfloat16 [81920, 128], P(('tm', 'feat'))
- surprise: float32 [81920], P(('tm', 'feat'))
Inputs may be any that keep to these rules, and one draw needn't show every extreme that they name: `span_of`: in each aligned block of 640 rows (the rows of one device) every span from 0 to 31 appears exactly 20 times.
All inputs are finite; a program needn't handle non-finite values.
Results may differ from a plain program's by a relative error of at most 0.0049.
Values may be sent and summed in bfloat16 or wider, within the bound.
No kernel may reach another device: no remote copies, remote signals or barrier semaphores. Data moves between devices by JAX's collectives and lax.ppermute only.
A program may use at most 320 MiB of HBM per device.

v0:
```python
import jax
import jax.numpy as jnp
from jax import lax
from jax.sharding import Mesh, PartitionSpec as P

ITERS = 3
RIDGE = 0.1
TINY = 1e-06
TM = ("x", "z", "c")
SWAP = [(0, 1), (1, 0)]


def masked_sum(stack, position):
    keep = jnp.arange(stack.shape[0]) < position
    return jnp.sum(jnp.where(keep.reshape((-1,) + (1,) * (stack.ndim - 1)), stack, 0.0), axis=0)


def exclusive_prefix(block):
    ci = lax.axis_index("c")
    zi = lax.axis_index("z")
    xi = lax.axis_index("x")
    rows = block.shape[0]
    half = rows // 2
    partner = lax.ppermute(block, "c", SWAP)
    chip = block + partner
    below = jnp.where(ci == 1, partner, 0.0)
    mine = lax.dynamic_slice_in_dim(chip, ci * half, half, 0)
    along_z = lax.all_gather(mine, "z")
    before_z = masked_sum(along_z, zi)
    total_z = jnp.sum(along_z, axis=0)
    along_x = lax.all_gather(total_z, "x")
    before_x = masked_sum(along_x, xi)
    mine_prefix = before_x + before_z
    other_prefix = lax.ppermute(mine_prefix, "c", SWAP)
    joined = jnp.zeros((rows,) + block.shape[1:], block.dtype)
    joined = lax.dynamic_update_slice_in_dim(joined, mine_prefix, ci * half, 0)
    joined = lax.dynamic_update_slice_in_dim(joined, other_prefix, (1 - ci) * half, 0)
    return joined + below


def body(activations, targets, span_of):
    spans = lax.axis_size(TM)
    feat_count = lax.axis_size("feat")
    tok_dev, width = activations.shape
    n_targets = targets.shape[1]
    block_rows = width // feat_count
    share = tok_dev // spans
    contract = (((0,), (0,)), ((), ()))
    highest = lax.Precision.HIGHEST
    order = jnp.argsort(span_of, stable=True)
    sorted_x = jnp.take(activations, order, axis=0).reshape(spans, share, width)
    sorted_y = jnp.take(targets, order, axis=0).reshape(spans, share, n_targets)
    moved_x, moved_y = (
        lax.all_to_all(sorted_x, TM, split_axis=0, concat_axis=0, tiled=True),
        lax.all_to_all(sorted_y, TM, split_axis=0, concat_axis=0, tiled=True),
    )
    local_x = moved_x.reshape(tok_dev, width)
    local_y = moved_y.reshape(tok_dev, n_targets)
    col_start = lax.axis_index("feat") * block_rows
    rows_x = lax.all_gather(local_x, "feat", axis=0, tiled=True)
    rows_y = lax.all_gather(local_y, "feat", axis=0, tiled=True)
    own = lax.dynamic_slice_in_dim(rows_x, col_start, block_rows, 1)
    gram_part = lax.dot_general(own, rows_x, contract, preferred_element_type=jnp.float32)
    cross_part = lax.dot_general(own, rows_y, contract, preferred_element_type=jnp.float32)
    gram_prefix = exclusive_prefix(gram_part)
    cross_prefix = exclusive_prefix(cross_part)
    span = (lax.axis_index("x") * lax.axis_size("z") + lax.axis_index("z")) * lax.axis_size(
        "c"
    ) + lax.axis_index("c")
    seen = (span * (tok_dev * feat_count)).astype(jnp.float32)
    scale = 1.0 / jnp.maximum(seen, 1.0)
    rhs = scale * cross_prefix

    def column_dot(left, right):
        return lax.psum(jnp.sum(left * right, axis=0), "feat")

    residual = rhs
    direction = rhs
    norm_now = column_dot(residual, residual)
    solution = None
    for step in range(ITERS):
        product = jnp.dot(
            gram_prefix,
            lax.all_gather(direction, "feat", axis=0, tiled=True),
            precision=highest,
            preferred_element_type=jnp.float32,
        )
        image = scale * product + RIDGE * direction
        alpha = norm_now / (column_dot(direction, image) + TINY)
        update = alpha * direction
        solution = update if solution is None else solution + update
        if step + 1 < ITERS:
            residual = residual - alpha * image
            norm_next = column_dot(residual, residual)
            direction = residual + norm_next / (norm_now + TINY) * direction
            norm_now = norm_next
    weights = lax.all_gather(solution.astype(jnp.bfloat16), "feat", axis=0, tiled=True)
    predicted = jnp.dot(local_x, weights, preferred_element_type=jnp.float32).astype(jnp.bfloat16)
    returned = lax.all_to_all(
        predicted.reshape(spans, share, n_targets), TM, split_axis=0, concat_axis=0, tiled=True
    )
    in_order = returned.reshape(tok_dev, n_targets)
    predictions = jnp.zeros_like(in_order).at[order].set(in_order)
    error = targets.astype(jnp.float32) - predictions.astype(jnp.float32)
    surprise = jnp.mean(error * error, axis=1)
    return (predictions, surprise)


def solution(mesh):
    tm = mesh.shape["tm"]
    feat = mesh.shape["feat"]
    fine = Mesh(mesh.devices.reshape(tm // 8, 4, 2, feat), TM + ("feat",))
    rows = TM + ("feat",)
    return jax.shard_map(
        body,
        mesh=fine,
        in_specs=(P(rows, None), P(rows, None), P(rows)),
        out_specs=(P(rows, None), P(rows)),
        check_vma=False,
    )
```

profile of v0, /device:TPU:1, one launch (start us, length us, event | category | flops | bytes accessed | tf_op | source)
XLA Modules:
  0.0 592.7 jit_solution(11710074773149398378)
XLA Ops:
  7.2 0.0 all-gather.11.cloned.1.call-start
  7.2 5.2 sort.17
  12.5 4.1 gather_fusion
  16.6 5.2 gather.13
  21.7 0.1 broadcast_in_dim.83
  21.9 2.2 broadcast_select_fusion
  24.1 48.7 %all_to_all.15 = bf16[32,20,2048]{2,1,0:T(8,128)(2,1)} all-to-all(bf16[32,20,2048]{2,1,0:T(8,128)(2,1)S(1)} %broadcast_select_fusion), channel_id=1, replica_groups=mesh['x'=4,'z'=4,'c'=2,'feat'=4] {'x','z','c'}, dimensions={0} | all-to-all | bytes 5242880 | tf_op jit(solution)/shard_map/all_to_all | solution.py:54
  72.8 5.2 reshape.51
  78.0 0.0 all-gather.11.cloned.1.call-update
  78.0 0.0 all-gather.19.cloned.1.call-start
  78.1 98.4 %all-gather.11.cloned.1.call-done = bf16[2560,2048]{1,0:T(8,128)(2,1)} async-done(((bf16[640,2048]{1,0:T(8,128)(2,1)}), bf16[2560,2048]{1,0:T(8,128)(2,1)}) %all-gather.11.cloned.1.call-update) | async-done | bytes 10485776 | tf_op jit(solution)/shard_map/all_gather | solution.py:60
  176.5 10.4 %fusion = f32[512,2048]{1,0:T(8,128)} fusion(bf16[2560,2048]{1,0:T(8,128)(2,1)} %all-gather.11.cloned.1.call-done, s32[]{:T(128)S(6)} %select_n.63), kind=kOutput, calls=%fused_computation.7 | convolution fusion | flops 5368709120 | bytes 17301508 | tf_op jit(solution)/shard_map/dot_general | solution.py:63
  186.9 0.8 collective-permute-start.2
  187.8 7.1 %collective-permute-done.2 = f32[512,2048]{1,0:T(8,128)} collective-permute-done((f32[512,2048]{1,0:T(8,128)}, f32[512,2048]{1,0:T(8,128)}, u32[]{:S(2)}, u32[]{:S(2)}) %collective-permute-start.2) | collective-permute-done | bytes 4194336 | tf_op jit(solution)/shard_map/ppermute | solution.py:24
  194.9 3.9 dynamic-slice_add_fusion
  198.9 0.0 all-gather.21.cloned.1.call-start
  198.9 83.9 %all-gather.19.cloned.1.call-done = f32[1024,2048]{1,0:T(8,128)} async-done(((f32[256,2048]{1,0:T(8,128)}), f32[1024,2048]{1,0:T(8,128)}) %all-gather.19.cloned.1.call-update) | async-done | bytes 8388624 | tf_op jit(solution)/shard_map/all_gather | solution.py:28
  282.8 6.5 %select_reduce_fusion = (f32[256,2048]{1,0:T(8,128)S(1)}, f32[256,2048]{1,0:T(8,128)}) fusion(f32[4,256,2048]{2,1,0:T(8,128)} %bitcast.14, pred[4]{0:T(512)(128)(4,1)S(1)} %iota_compare_fusion), kind=kLoop, calls=%fused_computation.3 | loop fusion | flops 5242880 | bytes 12582916 | tf_op jit(solution)/shard_map/reduce_sum | solution.py:15
  289.4 2.0 gather_fusion.1
  291.4 0.9 broadcast_select_fusion.1
  292.3 7.4 %all-to-all-start.1 = ((bf16[32,20,128]{2,1,0:T(8,128)(2,1)}), bf16[32,20,128]{2,1,0:T(8,128)(2,1)S(1)}, u32[]{:S(2)}, u32[]{:S(2)}) async-start(bf16[32,20,128]{2,1,0:T(8,128)(2,1)} %broadcast_select_fusion.1), calls=%async_computation.1 | async-start | bytes 393216 | tf_op jit(solution)/shard_map/all_to_all | solution.py:55
  299.7 0.0 all-gather.13.cloned.1.call-start
  299.7 8.2 %all-to-all-done.1 = bf16[32,20,128]{2,1,0:T(8,128)(2,1)S(1)} async-done(((bf16[32,20,128]{2,1,0:T(8,128)(2,1)}), bf16[32,20,128]{2,1,0:T(8,128)(2,1)S(1)}, u32[]{:S(2)}, u32[]{:S(2)}) %all-to-all-start.1) | async-done | bytes 163872 | tf_op jit(solution)/shard_map/all_to_all | solution.py:55
  308.0 11.8 %all_gather.43 = bf16[2560,128]{1,0:T(8,128)(2,1)S(1)} all-gather(bf16[640,128]{1,0:T(8,128)(2,1)S(1)} %reshape.52), channel_id=1, replica_groups=mesh['x'=4,'z'=4,'c'=2,'feat'=4] {'feat'}, dimensions={0}, use_global_device_ids=true | all-gather | bytes 819200 | tf_op jit(solution)/shard_map/all_gather | solution.py:61
  319.8 2.6 fusion.2
  322.4 2.1 collective-permute-start
  324.5 48.8 %all-gather.21.cloned.1.call-done = f32[1024,2048]{1,0:T(8,128)} async-done(((f32[256,2048]{1,0:T(8,128)}), f32[1024,2048]{1,0:T(8,128)}) %all-gather.21.cloned.1.call-update) | async-done | bytes 8388624 | tf_op jit(solution)/shard_map/all_gather | solution.py:31
  373.4 4.7 select_reduce_fusion.1
  378.1 2.5 broadcast_in_dim.92
  380.6 2.5 constant_dynamic-update-slice_fusion.1
  383.1 0.8 collective-permute-start.3
  383.9 11.2 %all-gather = f32[1024,128]{1,0:T(8,128)S(1)} all-gather(f32[256,128]{1,0:T(8,128)S(1)} %dynamic-slice_add_fusion.1), channel_id=2, replica_groups=mesh['x'=4,'z'=4,'c'=2,'feat'=4] {'z'}, dimensions={0}, use_global_device_ids=true | all-gather | bytes 655360 | tf_op jit(solution)/shard_map/all_gather | solution.py:28
  395.1 0.1 select_reduce_fusion.2
  395.2 10.4 %all-gather.1 = f32[1024,128]{1,0:T(8,128)S(1)} all-gather(f32[256,128]{1,0:T(8,128)S(1)} %get-tuple-element.7), channel_id=3, replica_groups=mesh['x'=4,'z'=4,'c'=2,'feat'=4] {'x'}, dimensions={0}, use_global_device_ids=true | all-gather | bytes 655360 | tf_op jit(solution)/shard_map/all_gather | solution.py:31
  405.6 0.1 select_reduce_fusion.3
  405.7 5.3 collective-permute-start.1
  411.1 0.9 collective-permute-done.1
  412.1 0.7 add_multiply_fusion
  412.8 0.0 all-gather.15.cloned.1.call-start
  412.9 1.6 constant_dynamic-update-slice_fusion
  414.4 6.6 %select_add_fusion = f32[512,2048]{1,0:T(8,128)} fusion(f32[512,2048]{1,0:T(8,128)} %constant_dynamic-update-slice_fusion, f32[512,2048]{1,0:T(8,128)} %collective-permute-done.2, pred[]{:T(512)S(6)} %eq.4), kind=kLoop, calls=%fused_computation.5 | loop fusion | flops 2097152 | bytes 12582913 | tf_op jit(solution)/shard_map/add | solution.py:38
  421.1 13.0 %all-gather.13.cloned.1.call-done = f32[2048,128]{1,0:T(8,128)} async-done(((f32[512,128]{1,0:T(8,128)}), f32[2048,128]{1,0:T(8,128)}) %all-gather.13.cloned.1.call-update) | async-done | bytes 1048592 | tf_op jit(solution)/shard_map/all_gather | solution.py:84
  434.1 5.5 multiply_reduce_fusion.4
  439.6 7.7 %all-reduce = (f32[128]{0:T(128)S(1)}, f32[128]{0:T(128)S(1)}) all-reduce(f32[128]{0:T(128)S(1)} %get-tuple-element.9, f32[128]{0:T(128)S(1)} %get-tuple-element.8), channel_id=1, replica_groups=mesh['x'=4,'z'=4,'c'=2,'feat'=4] {'feat'}, use_global_device_ids=true, to_apply=%region_5.6 | all-reduce | flops 256 | bytes 2048 | tf_op jit(solution)/shard_map/psum | solution.py:75
  447.3 0.1 multiply_reduce_fusion.3
  447.4 6.0 %psum.44 = f32[128]{0:T(128)S(1)} all-reduce(f32[128]{0:T(128)S(1)} %get-tuple-element.12), channel_id=1, replica_groups=mesh['x'=4,'z'=4,'c'=2,'feat'=4] {'feat'}, use_global_device_ids=true, to_apply=%region_12.13 | all-reduce | flops 128 | bytes 1024 | tf_op jit(solution)/shard_map/psum | solution.py:75
  453.4 0.7 multiply_add_fusion.1
  454.2 0.0 all-gather.17.cloned.1.call-start
  454.2 27.8 %all-gather.15.cloned.1.call-done = f32[2048,128]{1,0:T(8,128)} async-done(((f32[512,128]{1,0:T(8,128)}), f32[2048,128]{1,0:T(8,128)}) %all-gather.15.cloned.1.call-update) | async-done | bytes 1048592 | tf_op jit(solution)/shard_map/all_gather | solution.py:84
  482.0 5.9 %multiply_reduce_fusion.2 = (f32[128]{0:T(128)S(1)}, f32[512,128]{1,0:T(8,128)S(1)}) fusion(f32[512,128]{1,0:T(8,128)} %multiply_add_fusion.1, f32[512,2048]{1,0:T(8,128)} %select_add_fusion, f32[2048,128]{1,0:T(8,128)} %all-gather.15.cloned.1.call-done, f32[]{:T(128)S(6)} %div.24), kind=kOutput, calls=%fused_computation.28 | convolution fusion | flops 1610940288 | bytes 5767684 | tf_op jit(solution)/shard_map/dot_general | solution.py:82
  488.0 7.7 %psum.45 = f32[128]{0:T(128)S(1)} all-reduce(f32[128]{0:T(128)S(1)} %get-tuple-element.19), channel_id=1, replica_groups=mesh['x'=4,'z'=4,'c'=2,'feat'=4] {'feat'}, use_global_device_ids=true, to_apply=%region_14.15 | all-reduce | flops 128 | bytes 1024 | tf_op jit(solution)/shard_map/psum | solution.py:75
  495.7 0.1 multiply_reduce_fusion.1
  495.8 6.0 %psum.46 = f32[128]{0:T(128)S(1)} all-reduce(f32[128]{0:T(128)S(1)} %multiply_reduce_fusion.1), channel_id=1, replica_groups=mesh['x'=4,'z'=4,'c'=2,'feat'=4] {'feat'}, use_global_device_ids=true, to_apply=%region_16.17 | all-reduce | flops 128 | bytes 1024 | tf_op jit(solution)/shard_map/psum | solution.py:75
  501.8 0.8 multiply_add_fusion
  502.6 27.8 %all-gather.17.cloned.1.call-done = f32[2048,128]{1,0:T(8,128)} async-done(((f32[512,128]{1,0:T(8,128)}), f32[2048,128]{1,0:T(8,128)}) %all-gather.17.cloned.1.call-update) | async-done | bytes 1048592 | tf_op jit(solution)/shard_map/all_gather | solution.py:84
  530.4 6.1 %fusion.8 = f32[128]{0:T(128)S(1)} fusion(f32[512,128]{1,0:T(8,128)} %multiply_add_fusion, f32[512,2048]{1,0:T(8,128)} %select_add_fusion, f32[2048,128]{1,0:T(8,128)} %all-gather.17.cloned.1.call-done, f32[]{:T(128)S(6)} %div.24), kind=kOutput, calls=%fused_computation.20 | convolution fusion | flops 1610940288 | bytes 5505540 | tf_op jit(solution)/shard_map/dot_general | solution.py:82
  536.5 7.7 %psum.47 = f32[128]{0:T(128)S(1)} all-reduce(f32[128]{0:T(128)S(1)} %fusion.8), channel_id=1, replica_groups=mesh['x'=4,'z'=4,'c'=2,'feat'=4] {'feat'}, use_global_device_ids=true, to_apply=%region_18.19 | all-reduce | flops 128 | bytes 1024 | tf_op jit(solution)/shard_map/psum | solution.py:75
  544.2 1.0 add_convert_fusion
  545.2 10.8 %all_gather.55 = bf16[2048,128]{1,0:T(8,128)(2,1)S(1)} all-gather(bf16[512,128]{1,0:T(8,128)(2,1)S(1)} %add_convert_fusion), channel_id=1, replica_groups=mesh['x'=4,'z'=4,'c'=2,'feat'=4] {'feat'}, dimensions={0}, use_global_device_ids=true | all-gather | bytes 655360 | tf_op jit(solution)/shard_map/all_gather | solution.py:97
  556.0 2.6 convolution_convert_fusion
  558.6 22.2 %all_to_all.16 = bf16[32,20,128]{2,1,0:T(8,128)(2,1)S(1)} all-to-all(bf16[32,20,128]{2,1,0:T(8,128)(2,1)S(1)} %reshape.53), channel_id=1, replica_groups=mesh['x'=4,'z'=4,'c'=2,'feat'=4] {'x','z','c'}, dimensions={0} | all-to-all | bytes 327680 | tf_op jit(solution)/shard_map/all_to_all | solution.py:99
  580.8 4.3 scatter_custom_fusion
  585.1 0.2 multiply_reduce_fusion
  585.3 0.6 broadcast_multiply_fusion
  (38 shorter events, 0.4 us)
Async XLA Ops:
  7.2 5.3 copy-start
  7.2 169.3 %all-gather.11.cloned.1.call-start = ((), (), s32[]{:S(2)}) async-start(), calls=%async_computation.3 | async-start | bytes 13107200 | tf_op jit(solution)/shard_map/all_gather | solution.py:60
  78.0 204.8 %all-gather.19.cloned.1.call-start = ((), (), s32[]{:S(2)}) async-start(), calls=%async_computation.7 | async-start | bytes 10485760 | tf_op jit(solution)/shard_map/all_gather | solution.py:28
  186.9 8.0 %collective-permute-start.2 = (f32[512,2048]{1,0:T(8,128)}, f32[512,2048]{1,0:T(8,128)}, u32[]{:S(2)}, u32[]{:S(2)}) collective-permute-start(f32[512,2048]{1,0:T(8,128)} %fusion), channel_id=1, source_target_pairs={{0,4},{4,0},{1,5},{5,1},{2,6},{6,2},{3,7},{7,3},{8,12},{12,8},{9,1... | collective-permute-start | bytes 12582920 | tf_op jit(solution)/shard_map/ppermute | solution.py:24
  198.9 174.5 %all-gather.21.cloned.1.call-start = ((), (), s32[]{:S(2)}) async-start(), calls=%async_computation.8 | async-start | bytes 10485760 | tf_op jit(solution)/shard_map/all_gather | solution.py:31
  282.8 6.6 %copy-start.2 = (bf16[640,128]{1,0:T(8,128)(2,1)S(1)}, bf16[640,128]{1,0:T(8,128)(2,1)}, u32[]{:S(2)}) copy-start(bf16[640,128]{1,0:T(8,128)(2,1)} %param.4) | copy-start | bytes 491524
  292.3 15.7 %all-to-all-start.1 = ((bf16[32,20,128]{2,1,0:T(8,128)(2,1)}), bf16[32,20,128]{2,1,0:T(8,128)(2,1)S(1)}, u32[]{:S(2)}, u32[]{:S(2)}) async-start(bf16[32,20,128]{2,1,0:T(8,128)(2,1)} %broadcast_select_fusion.1), calls=%async_computation.1 | async-start | bytes 393216 | tf_op jit(solution)/shard_map/all_to_all | solution.py:55
  299.7 134.4 %all-gather.13.cloned.1.call-start = ((), (), s32[]{:S(2)}) async-start(), calls=%async_computation.4 | async-start | bytes 1310720 | tf_op jit(solution)/shard_map/all_gather | solution.py:84
  322.4 61.4 %collective-permute-start = (f32[512,128]{1,0:T(8,128)S(1)}, f32[512,128]{1,0:T(8,128)S(1)}, u32[]{:S(2)}, u32[]{:S(2)}) collective-permute-start(f32[512,128]{1,0:T(8,128)S(1)} %fusion.2), channel_id=1, source_target_pairs={{0,4},{4,0},{1,5},{5,1},{2,6},{6,2},{3,7},{7,3},{8,12},{12,8},{9,1... | collective-permute-start | bytes 786440 | tf_op jit(solution)/shard_map/ppermute | solution.py:24
  383.1 29.8 %collective-permute-start.3 = (f32[256,2048]{1,0:T(8,128)}, f32[256,2048]{1,0:T(8,128)S(1)}, u32[]{:S(2)}, u32[]{:S(2)}) collective-permute-start(f32[256,2048]{1,0:T(8,128)} %get-tuple-element.15), channel_id=1, source_target_pairs={{0,4},{4,0},{1,5},{5,1},{2,6},{6,2},{3,7},{7,3},{8,12},{12,8},{9,1... | collective-permute-start | bytes 6291464 | tf_op jit(solution)/shard_map/ppermute | solution.py:34
  405.7 6.3 %collective-permute-start.1 = (f32[256,128]{1,0:T(8,128)S(1)}, f32[256,128]{1,0:T(8,128)S(1)}, u32[]{:S(2)}, u32[]{:S(2)}) collective-permute-start(f32[256,128]{1,0:T(8,128)S(1)} %get-tuple-element.17), channel_id=1, source_target_pairs={{0,4},{4,0},{1,5},{5,1},{2,6},{6,2},{3,7},{7,3},{8,12},{12,8},{9,1... | collective-permute-start | bytes 393224 | tf_op jit(solution)/shard_map/ppermute | solution.py:34
  412.8 69.2 %all-gather.15.cloned.1.call-start = ((), (), s32[]{:S(2)}) async-start(), calls=%async_computation.5 | async-start | bytes 1310720 | tf_op jit(solution)/shard_map/all_gather | solution.py:84
  414.4 19.7 %copy-start.3 = (f32[512,128]{1,0:T(8,128)S(1)}, f32[512,128]{1,0:T(8,128)}, u32[]{:S(2)}) copy-start(f32[512,128]{1,0:T(8,128)} %add_multiply_fusion) | copy-start | bytes 786436
  454.2 47.6 %copy-start.4 = (f32[512,128]{1,0:T(8,128)S(1)}, f32[512,128]{1,0:T(8,128)}, u32[]{:S(2)}) copy-start(f32[512,128]{1,0:T(8,128)} %multiply_add_fusion.1) | copy-start | bytes 786436
  454.2 76.2 %all-gather.17.cloned.1.call-start = ((), (), s32[]{:S(2)}) async-start(), calls=%async_computation.6 | async-start | bytes 1310720 | tf_op jit(solution)/shard_map/all_gather | solution.py:84
  530.4 55.5 %copy-start.1 = (bf16[640,2048]{1,0:T(8,128)(2,1)S(1)}, bf16[640,2048]{1,0:T(8,128)(2,1)}, u32[]{:S(2)}) copy-start(bf16[640,2048]{1,0:T(8,128)(2,1)} %param.3) | copy-start | bytes 7864324
  585.1 0.8 copy-start.5
Sparse Core Ops, SparseCore 0:
  78.1 98.3 all-gather.10
  199.0 83.7 all-gather.18
  289.5 83.8 all-gather.20
  412.9 21.1 all-gather.12
  454.3 27.6 all-gather.14
  502.7 27.6 all-gather.16
where the time goes:
time: 594 us; the launch traced here: 593 us
  waiting for transfers between devices  316 us (53%)
  blocking collectives  150 us (25%)
  other arithmetic  37.2 us (6%)
  matrix products  33.2 us (6%)
  local copies, waits for them, and re-layouts  25.1 us (4%)
  starting transfers between devices  16.6 us (3%)
  between operations  14.4 us (2%)
    all_gather x1, waiting for transfers between devices, body(): rows_x = lax.all_gather(local_x, 'feat', axis=0, tiled=True)  98.4 us
    all_gather x1, waiting for transfers between devices, exclusive_prefix(): along_z = lax.all_gather(mine, 'z')  83.9 us
    all_gather x3, waiting for transfers between devices, body(): lax.all_gather(direction, 'feat', axis=0, tiled=True)  68.6 us
    all_gather x1, waiting for transfers between devices, exclusive_prefix(): along_x = lax.all_gather(total_z, 'x')  48.8 us
    all_to_all x1, blocking collectives, body(): lax.all_to_all(sorted_x, TM, split_axis=0, concat_axis=0, tiled=True)  48.7 us
    psum x5, blocking collectives, column_dot(): return lax.psum(jnp.sum(left * right, axis=0), 'feat')  35.1 us
    all_to_all x1, blocking collectives, body(): lax.all_to_all(predicted.reshape(spans, share, n_targets), TM, split_axis...  22.2 us
    dot_general x3, matrix products, body(): jnp.dot(gram_prefix, lax.all_gather(direction, 'feat', axis=0, tiled=True...  17.6 us
  transfers between devices with their start and end apart: 11, of which 9 were waited for; matrix products, arithmetic and copies ran while one was open for 4% of the time, Pallas kernels for 0%

commit v1 on v0

--- a/solution.py
+++ b/solution.py
@@ -8,6 +8,18 @@
 TINY = 1e-06
 TM = ("x", "z", "c")
 SWAP = [(0, 1), (1, 0)]
+
+
+def process_domain_for(original, net_axis):
+    return jnp.concatenate(
+        lax.all_to_all(
+            jnp.stack(lax.axis_size(net_axis) * [original]),
+            axis_name=net_axis,
+            split_axis=0,
+            concat_axis=0,
+        ),
+        axis=0,
+    )
 
 
 def masked_sum(stack, position):
@@ -57,7 +69,7 @@
     local_x = moved_x.reshape(tok_dev, width)
     local_y = moved_y.reshape(tok_dev, n_targets)
     col_start = lax.axis_index("feat") * block_rows
-    rows_x = lax.all_gather(local_x, "feat", axis=0, tiled=True)
+    rows_x = process_domain_for(local_x, "feat")
     rows_y = lax.all_gather(local_y, "feat", axis=0, tiled=True)
     own = lax.dynamic_slice_in_dim(rows_x, col_start, block_rows, 1)
     gram_part = lax.dot_general(own, rows_x, contract, preferred_element_type=jnp.float32)

time: 594 us -> 617 us (1.039)
  waiting for transfers between devices: 316 us -> 328 us
  starting transfers between devices: 16.6 us -> 22.9 us
    all_to_all x0 -> x1, waiting for transfers between devices: none -> 116 us  [process_domain_for(): lax.all_to_all(jnp.stack(lax.axis_size(net_axis) * [original]), axis_name...]
    all_gather x1 -> x0, waiting for transfers between devices: 98.4 us -> none  [body(): rows_x = lax.all_gather(local_x, 'feat', axis=0, tiled=True)]
where the time goes in v1:
time: 617 us; the launch traced here: 616 us
  waiting for transfers between devices  328 us (53%)
  blocking collectives  150 us (24%)
  other arithmetic  37.2 us (6%)
  matrix products  33.2 us (5%)
  local copies, waits for them, and re-layouts  28.8 us (5%)
  starting transfers between devices  22.9 us (4%)
  between operations  16 us (3%)
    all_to_all x1, waiting for transfers between devices, process_domain_for(): lax.all_to_all(jnp.stack(lax.axis_size(net_axis) * [original]), axis_name...  116 us
    all_gather x1, waiting for transfers between devices, exclusive_prefix(): along_z = lax.all_gather(mine, 'z')  78.8 us
    all_gather x3, waiting for transfers between devices, body(): lax.all_gather(direction, 'feat', axis=0, tiled=True)  68.2 us
    all_to_all x1, blocking collectives, body(): lax.all_to_all(sorted_x, TM, split_axis=0, concat_axis=0, tiled=True)  48.7 us
    all_gather x1, waiting for transfers between devices, exclusive_prefix(): along_x = lax.all_gather(total_z, 'x')  48.7 us
    psum x5, blocking collectives, column_dot(): return lax.psum(jnp.sum(left * right, axis=0), 'feat')  35.4 us
    all_to_all x1, blocking collectives, body(): lax.all_to_all(predicted.reshape(spans, share, n_targets), TM, split_axis...  22.1 us
    dot_general x3, matrix products, body(): jnp.dot(gram_prefix, lax.all_gather(direction, 'feat', axis=0, tiled=True...  17.6 us
  transfers between devices with their start and end apart: 11, of which 9 were waited for; matrix products, arithmetic and copies ran while one was open for 4% of the time, Pallas kernels for 0%

profile of v1, /device:TPU:1, one launch (start us, length us, event | category | flops | bytes accessed | tf_op | source)
XLA Modules:
  0.0 616.4 jit_solution(5379185059910112236)
XLA Ops:
  8.0 5.2 sort.17
  13.3 4.1 gather_fusion
  17.4 5.2 gather.13
  22.5 0.1 broadcast_in_dim.83
  22.6 2.2 broadcast_select_fusion
  24.9 48.7 %all_to_all.20 = bf16[32,20,2048]{2,1,0:T(8,128)(2,1)} all-to-all(bf16[32,20,2048]{2,1,0:T(8,128)(2,1)S(1)} %broadcast_select_fusion), channel_id=1, replica_groups=mesh['x'=4,'z'=4,'c'=2,'feat'=4] {'x','z','c'}, dimensions={0} | all-to-all | bytes 5242880 | tf_op jit(solution)/shard_map/all_to_all | solution.py:66
  73.6 3.6 reshape.56
  77.3 5.3 stack.3
  82.5 6.0 all-to-all-start.1
  88.5 0.0 all-gather.16.cloned.1.call-start
  88.6 116.2 %all-to-all-done.1 = bf16[4,640,2048]{2,1,0:T(8,128)(2,1)} async-done(((bf16[4,640,2048]{2,1,0:T(8,128)(2,1)}), bf16[4,640,2048]{2,1,0:T(8,128)(2,1)}, u32[]{:S(2)}, u32[]{:S(2)}) %all-to-all-start.1) | async-done | bytes 10485792 | tf_op jit(solution)/shard_map/all_to_all | solution.py:15
  204.8 10.4 %fusion = f32[512,2048]{1,0:T(8,128)} fusion(bf16[2560,2048]{1,0:T(8,128)(2,1)} %bitcast, s32[]{:T(128)S(6)} %select_n.63), kind=kOutput, calls=%fused_computation.7 | convolution fusion | flops 5368709120 | bytes 17301508 | tf_op jit(solution)/shard_map/dot_general | solution.py:75
  215.2 1.0 collective-permute-start.2
  216.2 7.1 %collective-permute-done.2 = f32[512,2048]{1,0:T(8,128)} collective-permute-done((f32[512,2048]{1,0:T(8,128)}, f32[512,2048]{1,0:T(8,128)}, u32[]{:S(2)}, u32[]{:S(2)}) %collective-permute-start.2) | collective-permute-done | bytes 4194336 | tf_op jit(solution)/shard_map/ppermute | solution.py:36
  223.3 3.9 dynamic-slice_add_fusion
  227.2 0.0 all-gather.18.cloned.1.call-start
  227.3 78.8 %all-gather.16.cloned.1.call-done = f32[1024,2048]{1,0:T(8,128)} async-done(((f32[256,2048]{1,0:T(8,128)}), f32[1024,2048]{1,0:T(8,128)}) %all-gather.16.cloned.1.call-update) | async-done | bytes 8388624 | tf_op jit(solution)/shard_map/all_gather | solution.py:40
  306.1 6.5 %select_reduce_fusion = (f32[256,2048]{1,0:T(8,128)S(1)}, f32[256,2048]{1,0:T(8,128)}) fusion(f32[4,256,2048]{2,1,0:T(8,128)} %bitcast.15, pred[4]{0:T(512)(128)(4,1)S(1)} %iota_compare_fusion), kind=kLoop, calls=%fused_computation.3 | loop fusion | flops 5242880 | bytes 12582916 | tf_op jit(solution)/shard_map/reduce_sum | solution.py:27
  312.7 2.0 gather_fusion.1
  314.7 0.9 broadcast_select_fusion.1
  315.6 7.4 %all-to-all-start.2 = ((bf16[32,20,128]{2,1,0:T(8,128)(2,1)}), bf16[32,20,128]{2,1,0:T(8,128)(2,1)S(1)}, u32[]{:S(2)}, u32[]{:S(2)}) async-start(bf16[32,20,128]{2,1,0:T(8,128)(2,1)} %broadcast_select_fusion.1), calls=%async_computation.2 | async-start | bytes 393216 | tf_op jit(solution)/shard_map/all_to_all | solution.py:67
  323.0 0.0 all-gather.10.cloned.1.call-start
  323.1 8.2 %all-to-all-done.2 = bf16[32,20,128]{2,1,0:T(8,128)(2,1)S(1)} async-done(((bf16[32,20,128]{2,1,0:T(8,128)(2,1)}), bf16[32,20,128]{2,1,0:T(8,128)(2,1)S(1)}, u32[]{:S(2)}, u32[]{:S(2)}) %all-to-all-start.2) | async-done | bytes 163872 | tf_op jit(solution)/shard_map/all_to_all | solution.py:67
  331.3 11.8 %all_gather.39 = bf16[2560,128]{1,0:T(8,128)(2,1)S(1)} all-gather(bf16[640,128]{1,0:T(8,128)(2,1)S(1)} %reshape.58), channel_id=1, replica_groups=mesh['x'=4,'z'=4,'c'=2,'feat'=4] {'feat'}, dimensions={0}, use_global_device_ids=true | all-gather | bytes 819200 | tf_op jit(solution)/shard_map/all_gather | solution.py:73
  343.1 2.6 fusion.2
  345.8 2.2 collective-permute-start
  348.0 48.7 %all-gather.18.cloned.1.call-done = f32[1024,2048]{1,0:T(8,128)} async-done(((f32[256,2048]{1,0:T(8,128)}), f32[1024,2048]{1,0:T(8,128)}) %all-gather.18.cloned.1.call-update) | async-done | bytes 8388624 | tf_op jit(solution)/shard_map/all_gather | solution.py:43
  396.7 4.7 select_reduce_fusion.1
  401.4 2.5 broadcast_in_dim.92
  403.9 2.5 constant_dynamic-update-slice_fusion.1
  406.4 0.8 collective-permute-start.3
  407.2 11.2 %all-gather = f32[1024,128]{1,0:T(8,128)S(1)} all-gather(f32[256,128]{1,0:T(8,128)S(1)} %dynamic-slice_add_fusion.1), channel_id=2, replica_groups=mesh['x'=4,'z'=4,'c'=2,'feat'=4] {'z'}, dimensions={0}, use_global_device_ids=true | all-gather | bytes 655360 | tf_op jit(solution)/shard_map/all_gather | solution.py:40
  418.4 0.1 select_reduce_fusion.2
  418.5 10.4 %all-gather.1 = f32[1024,128]{1,0:T(8,128)S(1)} all-gather(f32[256,128]{1,0:T(8,128)S(1)} %get-tuple-element.7), channel_id=3, replica_groups=mesh['x'=4,'z'=4,'c'=2,'feat'=4] {'x'}, dimensions={0}, use_global_device_ids=true | all-gather | bytes 655360 | tf_op jit(solution)/shard_map/all_gather | solution.py:43
  428.9 0.1 select_reduce_fusion.3
  429.1 5.3 collective-permute-start.1
  434.4 0.9 collective-permute-done.1
  435.4 0.7 add_multiply_fusion
  436.1 0.0 all-gather.12.cloned.1.call-start
  436.2 1.6 constant_dynamic-update-slice_fusion
  437.8 6.6 %select_add_fusion = f32[512,2048]{1,0:T(8,128)} fusion(f32[512,2048]{1,0:T(8,128)} %constant_dynamic-update-slice_fusion, f32[512,2048]{1,0:T(8,128)} %collective-permute-done.2, pred[]{:T(512)S(6)} %eq.4), kind=kLoop, calls=%fused_computation.5 | loop fusion | flops 2097152 | bytes 12582913 | tf_op jit(solution)/shard_map/add | solution.py:50
  444.4 12.9 %all-gather.10.cloned.1.call-done = f32[2048,128]{1,0:T(8,128)} async-done(((f32[512,128]{1,0:T(8,128)}), f32[2048,128]{1,0:T(8,128)}) %all-gather.10.cloned.1.call-update) | async-done | bytes 1048592 | tf_op jit(solution)/shard_map/all_gather | solution.py:96
  457.3 5.5 multiply_reduce_fusion.4
  462.8 7.7 %all-reduce = (f32[128]{0:T(128)S(1)}, f32[128]{0:T(128)S(1)}) all-reduce(f32[128]{0:T(128)S(1)} %get-tuple-element.9, f32[128]{0:T(128)S(1)} %get-tuple-element.8), channel_id=1, replica_groups=mesh['x'=4,'z'=4,'c'=2,'feat'=4] {'feat'}, use_global_device_ids=true, to_apply=%region_5.6 | all-reduce | flops 256 | bytes 2048 | tf_op jit(solution)/shard_map/psum | solution.py:87
  470.6 0.1 multiply_reduce_fusion.3
  470.7 6.0 psum.44
  476.7 0.7 multiply_add_fusion.1
  477.4 0.0 all-gather.14.cloned.1.call-start
  477.5 27.6 %all-gather.12.cloned.1.call-done = f32[2048,128]{1,0:T(8,128)} async-done(((f32[512,128]{1,0:T(8,128)}), f32[2048,128]{1,0:T(8,128)}) %all-gather.12.cloned.1.call-update) | async-done | bytes 1048592 | tf_op jit(solution)/shard_map/all_gather | solution.py:96
  505.1 5.9 multiply_reduce_fusion.2
  511.1 7.7 %psum.45 = f32[128]{0:T(128)S(1)} all-reduce(f32[128]{0:T(128)S(1)} %get-tuple-element.19), channel_id=1, replica_groups=mesh['x'=4,'z'=4,'c'=2,'feat'=4] {'feat'}, use_global_device_ids=true, to_apply=%region_14.15 | all-reduce | flops 128 | bytes 1024 | tf_op jit(solution)/shard_map/psum | solution.py:87
  518.8 0.1 multiply_reduce_fusion.1
  518.9 6.2 %psum.46 = f32[128]{0:T(128)S(1)} all-reduce(f32[128]{0:T(128)S(1)} %multiply_reduce_fusion.1), channel_id=1, replica_groups=mesh['x'=4,'z'=4,'c'=2,'feat'=4] {'feat'}, use_global_device_ids=true, to_apply=%region_16.17 | all-reduce | flops 128 | bytes 1024 | tf_op jit(solution)/shard_map/psum | solution.py:87
  525.1 0.8 multiply_add_fusion
  525.9 27.7 %all-gather.14.cloned.1.call-done = f32[2048,128]{1,0:T(8,128)} async-done(((f32[512,128]{1,0:T(8,128)}), f32[2048,128]{1,0:T(8,128)}) %all-gather.14.cloned.1.call-update) | async-done | bytes 1048592 | tf_op jit(solution)/shard_map/all_gather | solution.py:96
  553.6 6.1 fusion.8
  559.7 7.7 %psum.47 = f32[128]{0:T(128)S(1)} all-reduce(f32[128]{0:T(128)S(1)} %fusion.8), channel_id=1, replica_groups=mesh['x'=4,'z'=4,'c'=2,'feat'=4] {'feat'}, use_global_device_ids=true, to_apply=%region_18.19 | all-reduce | flops 128 | bytes 1024 | tf_op jit(solution)/shard_map/psum | solution.py:87
  567.4 1.0 add_convert_fusion
  568.4 10.5 %all_gather.51 = bf16[2048,128]{1,0:T(8,128)(2,1)S(1)} all-gather(bf16[512,128]{1,0:T(8,128)(2,1)S(1)} %add_convert_fusion), channel_id=1, replica_groups=mesh['x'=4,'z'=4,'c'=2,'feat'=4] {'feat'}, dimensions={0}, use_global_device_ids=true | all-gather | bytes 655360 | tf_op jit(solution)/shard_map/all_gather | solution.py:109
  578.9 2.6 convolution_convert_fusion
  581.6 22.1 %all_to_all.21 = bf16[32,20,128]{2,1,0:T(8,128)(2,1)S(1)} all-to-all(bf16[32,20,128]{2,1,0:T(8,128)(2,1)S(1)} %reshape.59), channel_id=1, replica_groups=mesh['x'=4,'z'=4,'c'=2,'feat'=4] {'x','z','c'}, dimensions={0} | all-to-all | bytes 327680 | tf_op jit(solution)/shard_map/all_to_all | solution.py:111
  603.8 4.3 scatter_custom_fusion
  608.1 0.2 multiply_reduce_fusion
  608.2 0.6 broadcast_multiply_fusion
  (40 shorter events, 0.4 us)
Async XLA Ops:
  8.0 5.3 copy-start
  77.2 5.3 copy-start.3
  82.5 122.3 %all-to-all-start.1 = ((bf16[4,640,2048]{2,1,0:T(8,128)(2,1)}), bf16[4,640,2048]{2,1,0:T(8,128)(2,1)}, u32[]{:S(2)}, u32[]{:S(2)}) async-start(bf16[4,640,2048]{2,1,0:T(8,128)(2,1)} %stack.3), calls=%async_computation.1 | async-start | bytes 20971520 | tf_op jit(solution)/shard_map/all_to_all | solution.py:15
  88.5 217.6 %all-gather.16.cloned.1.call-start = ((), (), s32[]{:S(2)}) async-start(), calls=%async_computation.7 | async-start | bytes 10485760 | tf_op jit(solution)/shard_map/all_gather | solution.py:40
  215.2 8.1 %collective-permute-start.2 = (f32[512,2048]{1,0:T(8,128)}, f32[512,2048]{1,0:T(8,128)}, u32[]{:S(2)}, u32[]{:S(2)}) collective-permute-start(f32[512,2048]{1,0:T(8,128)} %fusion), channel_id=1, source_target_pairs={{0,4},{4,0},{1,5},{5,1},{2,6},{6,2},{3,7},{7,3},{8,12},{12,8},{9,1... | collective-permute-start | bytes 12582920 | tf_op jit(solution)/shard_map/ppermute | solution.py:36
  227.2 169.4 %all-gather.18.cloned.1.call-start = ((), (), s32[]{:S(2)}) async-start(), calls=%async_computation.8 | async-start | bytes 10485760 | tf_op jit(solution)/shard_map/all_gather | solution.py:43
  306.1 6.6 %copy-start.2 = (bf16[640,128]{1,0:T(8,128)(2,1)S(1)}, bf16[640,128]{1,0:T(8,128)(2,1)}, u32[]{:S(2)}) copy-start(bf16[640,128]{1,0:T(8,128)(2,1)} %param.4) | copy-start | bytes 491524
  315.6 15.7 %all-to-all-start.2 = ((bf16[32,20,128]{2,1,0:T(8,128)(2,1)}), bf16[32,20,128]{2,1,0:T(8,128)(2,1)S(1)}, u32[]{:S(2)}, u32[]{:S(2)}) async-start(bf16[32,20,128]{2,1,0:T(8,128)(2,1)} %broadcast_select_fusion.1), calls=%async_computation.2 | async-start | bytes 393216 | tf_op jit(solution)/shard_map/all_to_all | solution.py:67
  323.0 134.3 %all-gather.10.cloned.1.call-start = ((), (), s32[]{:S(2)}) async-start(), calls=%async_computation.4 | async-start | bytes 1310720 | tf_op jit(solution)/shard_map/all_gather | solution.py:96
  345.8 61.4 %collective-permute-start = (f32[512,128]{1,0:T(8,128)S(1)}, f32[512,128]{1,0:T(8,128)S(1)}, u32[]{:S(2)}, u32[]{:S(2)}) collective-permute-start(f32[512,128]{1,0:T(8,128)S(1)} %fusion.2), channel_id=1, source_target_pairs={{0,4},{4,0},{1,5},{5,1},{2,6},{6,2},{3,7},{7,3},{8,12},{12,8},{9,1... | collective-permute-start | bytes 786440 | tf_op jit(solution)/shard_map/ppermute | solution.py:36
  406.4 29.8 %collective-permute-start.3 = (f32[256,2048]{1,0:T(8,128)}, f32[256,2048]{1,0:T(8,128)S(1)}, u32[]{:S(2)}, u32[]{:S(2)}) collective-permute-start(f32[256,2048]{1,0:T(8,128)} %get-tuple-element.15), channel_id=1, source_target_pairs={{0,4},{4,0},{1,5},{5,1},{2,6},{6,2},{3,7},{7,3},{8,12},{12,8},{9,1... | collective-permute-start | bytes 6291464 | tf_op jit(solution)/shard_map/ppermute | solution.py:46
  429.1 6.3 %collective-permute-start.1 = (f32[256,128]{1,0:T(8,128)S(1)}, f32[256,128]{1,0:T(8,128)S(1)}, u32[]{:S(2)}, u32[]{:S(2)}) collective-permute-start(f32[256,128]{1,0:T(8,128)S(1)} %get-tuple-element.17), channel_id=1, source_target_pairs={{0,4},{4,0},{1,5},{5,1},{2,6},{6,2},{3,7},{7,3},{8,12},{12,8},{9,1... | collective-permute-start | bytes 393224 | tf_op jit(solution)/shard_map/ppermute | solution.py:46
  436.1 69.0 %all-gather.12.cloned.1.call-start = ((), (), s32[]{:S(2)}) async-start(), calls=%async_computation.5 | async-start | bytes 1310720 | tf_op jit(solution)/shard_map/all_gather | solution.py:96
  437.8 19.5 %copy-start.4 = (f32[512,128]{1,0:T(8,128)S(1)}, f32[512,128]{1,0:T(8,128)}, u32[]{:S(2)}) copy-start(f32[512,128]{1,0:T(8,128)} %add_multiply_fusion) | copy-start | bytes 786436
  477.4 47.7 %copy-start.5 = (f32[512,128]{1,0:T(8,128)S(1)}, f32[512,128]{1,0:T(8,128)}, u32[]{:S(2)}) copy-start(f32[512,128]{1,0:T(8,128)} %multiply_add_fusion.1) | copy-start | bytes 786436
  477.4 76.1 %all-gather.14.cloned.1.call-start = ((), (), s32[]{:S(2)}) async-start(), calls=%async_computation.6 | async-start | bytes 1310720 | tf_op jit(solution)/shard_map/all_gather | solution.py:96
  553.6 55.3 %copy-start.1 = (bf16[640,2048]{1,0:T(8,128)(2,1)S(1)}, bf16[640,2048]{1,0:T(8,128)(2,1)}, u32[]{:S(2)}) copy-start(bf16[640,2048]{1,0:T(8,128)(2,1)} %param.3) | copy-start | bytes 7864324
  608.0 0.8 copy-start.6
Sparse Core Ops, SparseCore 0:
  227.4 78.7 all-gather.15
  312.8 83.8 all-gather.17
Sparse Core Ops, SparseCore 1:
  436.2 21.0 all-gather.9
  477.5 27.5 all-gather.11
  526.0 27.5 all-gather.13
